TPU v7x, 512 devices: a whole 4x8x8 slice. The times are simulated.
512 devices in a mesh: dp: 16 (over z, core), expert: 32 (over x, y).
Axes of the slice: x: 4, y: 8, z: 8, core: 2. Of those that a mesh axis runs over, the one named last changes fastest.
Arguments:
- residual_in: bfloat16 [16384, 2048], P(('dp', 'expert')), may hold values from -6 to 6
- attention_out: bfloat16 [16384, 2048], P(('dp', 'expert')), may hold values from -6 to 6
- out_weight: bfloat16 [2048, 2048], P(None, 'dp'), may hold values from -0.125 to 0.125
- post_gain: float32 [2048], replicated, may hold values from 0.1 to 1.9
- router_weight: bfloat16 [2048, 32], replicated, may hold values from -0.125 to 0.125
- expert_ids: int32 [16384, 6], P(('dp', 'expert')), may hold values from 0 to 31, all different within a row; in each aligned block of 32 rows (0 to 31, 32 to 63, ...) at most 12 rows name the same one
- expert_slot: int32 [32], replicated, may hold values from 0 to 31, each once
- expert_gate_up: bfloat16 [32, 2048, 1408], P('expert', 'dp'), may hold values from -0.125 to 0.125
- expert_down: bfloat16 [32, 704, 2048], P('expert', None, 'dp'), may hold values from -0.21875 to 0.21875
- shared_gate_up: bfloat16 [2048, 2, 2816], P(None, None, 'dp'), may hold values from -0.125 to 0.125
- shared_down: bfloat16 [2816, 2048], P(None, 'dp'), may hold values from -0.109375 to 0.109375
- final_gain: float32 [2048], replicated, may hold values from 0.1 to 1.9
Outputs:
- mixed: bfloat16 [16384, 2048], P(('dp', 'expert'))
Inputs may be any that keep to these rules, and one draw needn't show every extreme that they name: `expert_ids`: each row names 6 different experts. In each aligned block of 32 rows (the rows of one device) no expert is named by more than 12 rows, a bound that some block reaches. A permutation: expert e is held in slot expert_slot[e].
All inputs are finite; a program needn't handle non-finite values.
Results may differ from a plain program's by a relative error of at most 0.0069.
Values may be sent and summed in bfloat16 or wider, within the bound.
No kernel may reach another device: no remote copies, remote signals or barrier semaphores. Data moves between devices by JAX's collectives and lax.ppermute only.
A program may use at most 64 MiB of HBM per device.

v0:
```python
import jax
import jax.numpy as jnp
from jax import lax
from jax.sharding import PartitionSpec as P

EPS = 1e-06


def in_order(blocks, dim):
    shape = list(blocks.shape[1:])
    shape[dim] *= blocks.shape[0]
    return jnp.moveaxis(blocks, 0, dim).reshape(shape)


def sent_to_all(array, axis):
    copies = jnp.broadcast_to(array, (lax.axis_size(axis), *array.shape))
    return lax.all_to_all(copies, axis, split_axis=0, concat_axis=0, tiled=True)


def collect(array, axis, dim):
    return in_order(sent_to_all(array, axis), dim)


def turned_gather(arrays, axis, dims):
    turned = [jnp.moveaxis(a, dim, 0) for a, dim in zip(arrays, dims)]
    widths = [t[0].size for t in turned]
    both = jnp.concatenate([t.reshape(-1, w) for t, w in zip(turned, widths)], axis=1)
    out = lax.all_gather(both, axis, axis=0, tiled=True)
    blocks = jnp.split(out, [sum(widths[:k]) for k in range(1, len(widths))], axis=1)
    return tuple(
        (
            jnp.moveaxis(b.reshape(-1, *t.shape[1:]), 0, dim)
            for b, t, dim in zip(blocks, turned, dims)
        )
    )


def rms_scale(values, gain):
    values = values.astype(jnp.float32)
    inverse = lax.rsqrt(jnp.mean(values * values, axis=-1, keepdims=True) + EPS)
    return values * inverse * gain


def per_device(
    residual_in,
    attention_out,
    out_weight,
    post_gain,
    router_weight,
    expert_ids,
    expert_slot,
    expert_gate_up,
    expert_down,
    shared_gate_up,
    shared_down,
    final_gain,
):
    rows = residual_in.shape[0]
    width = residual_in.shape[1]
    experts = router_weight.shape[1]
    choose = expert_ids.shape[1]
    capacity = max(2, min(rows, 2 * rows * choose // experts))
    proj_cols = jnp.dot(
        collect(attention_out, "dp", 0), out_weight, preferred_element_type=jnp.float32
    ).astype(jnp.bfloat16)
    proj = lax.all_to_all(proj_cols, "dp", split_axis=0, concat_axis=1, tiled=True)
    resid = (residual_in.astype(jnp.float32) + proj.astype(jnp.float32)).astype(jnp.bfloat16)
    normed = rms_scale(resid, post_gain).astype(jnp.bfloat16)
    logits = jnp.dot(normed, router_weight, preferred_element_type=jnp.float32)
    expert_range = jnp.arange(experts, dtype=jnp.int32)
    picked = expert_ids[:, :, None] == expert_range[None, None, :]
    chosen = jnp.sum(jnp.where(picked, logits[:, None, :], 0.0), axis=2)
    raised = jnp.exp(chosen)
    gates = raised / jnp.sum(raised, axis=1, keepdims=True)
    slots = jnp.sum(jnp.where(picked, expert_slot[None, None, :], 0), axis=2).reshape(-1)
    marked = (slots[:, None] == expert_range[None, :]).astype(jnp.int32)
    before = jnp.cumsum(marked, axis=0) - marked
    position = jnp.sum(before * marked, axis=1)
    target = slots * capacity + position
    placed = target[:, None] == jnp.arange(experts * capacity, dtype=jnp.int32)[None, :]
    select = jnp.any(placed.reshape(rows, choose, experts * capacity), axis=1).astype(jnp.bfloat16)
    outgoing = jnp.einsum("rs,rd->sd", select, normed, preferred_element_type=jnp.float32)
    outgoing = outgoing.astype(jnp.bfloat16).reshape(experts, capacity, width)
    gate_up_all, down_all = turned_gather((expert_gate_up, expert_down), "dp", (1, 2))
    gate_up_full = gate_up_all[0]
    down_full = down_all[0]
    hidden_units = gate_up_full.shape[1] // 2
    received = lax.all_to_all(outgoing, "expert", split_axis=0, concat_axis=0, tiled=True)
    sources, count, _ = received.shape
    flat = received.reshape(sources * count, width)
    both = jnp.dot(flat, gate_up_full, preferred_element_type=jnp.float32)
    active = (jax.nn.silu(both[:, :hidden_units]) * both[:, hidden_units:]).astype(jnp.bfloat16)
    result = jnp.dot(active, down_full, preferred_element_type=jnp.float32).astype(jnp.bfloat16)
    result = result.reshape(sources, count, width)
    returned = lax.all_to_all(result, "expert", split_axis=0, concat_axis=0, tiled=True)
    shared_units = shared_gate_up.shape[2]
    shared_pair = shared_gate_up.reshape(width, 2 * shared_units)
    both = jnp.dot(
        lax.all_gather(normed, "dp", axis=0, tiled=True),
        shared_pair,
        preferred_element_type=jnp.float32,
    )
    shared_hidden = (jax.nn.silu(both[:, :shared_units]) * both[:, shared_units:]).astype(
        jnp.bfloat16
    )
    out_cols = jnp.dot(
        lax.all_gather(shared_hidden, "dp", axis=1, tiled=True),
        shared_down,
        preferred_element_type=jnp.float32,
    )
    shared_out = lax.all_to_all(out_cols, "dp", split_axis=0, concat_axis=1, tiled=True)
    back_rows = jnp.take(returned.reshape(experts * capacity, width), target, axis=0)
    back_rows = back_rows.reshape(rows, choose, width).astype(jnp.float32)
    routed = jnp.sum(gates[:, :, None] * back_rows, axis=1)
    total = resid.astype(jnp.float32) + routed + shared_out
    return rms_scale(total, final_gain).astype(jnp.bfloat16)


def solution(mesh):
    in_specs = (
        P(("dp", "expert"), None),
        P(("dp", "expert"), None),
        P(None, "dp"),
        P(),
        P(),
        P(("dp", "expert"), None),
        P(),
        P("expert", "dp", None),
        P("expert", None, "dp"),
        P(None, None, "dp"),
        P(None, "dp"),
        P(),
    )
    out_specs = P(("dp", "expert"), None)
    return jax.shard_map(
        per_device, mesh=mesh, in_specs=in_specs, out_specs=out_specs, check_vma=False
    )
```

profile of v0, /device:TPU:1, one launch (start us, length us, event | category | flops | bytes accessed | tf_op | source)
XLA Modules:
  0.0 282.8 jit_solution(13538233987763280168)
XLA Ops:
  7.8 62.8 %all_to_all.47 = bf16[16,32,2048]{2,1,0:T(8,128)(2,1)S(1)} all-to-all(bf16[16,32,2048]{2,1,0:T(8,128)(2,1)S(1)} %broadcast_in_dim.50), channel_id=1, replica_groups=mesh['dp'=16,'expert'=32] {'dp'}, dimensions={0} | all-to-all | bytes 4194304 | tf_op jit(solution)/shard_map/all_to_all | solution.py:17
  71.4 11.9 %all_to_all.48 = bf16[16,32,128]{2,1,0:T(8,128)(2,1)S(1)} all-to-all(bf16[16,32,128]{2,1,0:T(8,128)(2,1)S(1)} %bitcast.66), channel_id=1, replica_groups=mesh['dp'=16,'expert'=32] {'dp'}, dimensions={0} | all-to-all | bytes 262144 | tf_op jit(solution)/shard_map/all_to_all | solution.py:66
  88.9 1.6 reshape.147
  90.6 9.7 %all-to-all-start.2 = ((bf16[32,12,2048]{2,1,0:T(8,128)(2,1)}), bf16[32,12,2048]{2,1,0:T(8,128)(2,1)S(1)}, u32[]{:S(2)}, u32[]{:S(2)}) async-start(bf16[32,12,2048]{2,1,0:T(8,128)(2,1)} %reshape.147), calls=%async_computation.2 | async-start | bytes 4194304 | tf_op jit(solution)/shard_map/all_to_all | solution.py:88
  100.3 24.4 %all-gather.6.cloned.1.call-done = bf16[512,2048]{1,0:T(8,128)(2,1)} async-done(((bf16[32,2048]{1,0:T(8,128)(2,1)}), bf16[512,2048]{1,0:T(8,128)(2,1)}) %all-gather.6.cloned.1.call-update) | async-done | bytes 2097168 | tf_op jit(solution)/shard_map/all_gather | solution.py:99
  124.7 2.5 fusion.21
  128.1 22.2 %all-to-all-done.2 = bf16[32,12,2048]{2,1,0:T(8,128)(2,1)S(1)} async-done(((bf16[32,12,2048]{2,1,0:T(8,128)(2,1)}), bf16[32,12,2048]{2,1,0:T(8,128)(2,1)S(1)}, u32[]{:S(2)}, u32[]{:S(2)}) %all-to-all-start.2) | async-done | bytes 1572896 | tf_op jit(solution)/shard_map/all_to_all | solution.py:88
  150.2 1.4 reshape.148
  151.7 35.1 %all-gather.4.cloned.1.call-done = bf16[2048,2112]{1,0:T(8,128)(2,1)} async-done(((bf16[128,2112]{1,0:T(8,128)(2,1)}), bf16[2048,2112]{1,0:T(8,128)(2,1)}) %all-gather.4.cloned.1.call-update) | async-done | bytes 8650768 | tf_op jit(solution)/shard_map/all_gather | solution.py:28
  186.8 5.7 %fusion = f32[384,1408]{1,0:T(8,128)S(1)} fusion(bf16[384,2048]{1,0:T(8,128)(2,1)} %reshape.148, bf16[2048,2112]{1,0:T(8,128)(2,1)} %all-gather.4.cloned.1.call-done), kind=kOutput, calls=%fused_computation.1 | convolution fusion | flops 2214592512 | bytes 9502720 | tf_op jit(solution)/shard_map/dot_general | solution.py:91
  192.5 3.3 %fusion.3 = bf16[384,2048]{1,0:T(8,128)(2,1)S(1)} fusion(bf16[2048,2112]{1,0:T(8,128)(2,1)} %all-gather.4.cloned.1.call-done, f32[384,1408]{1,0:T(8,128)S(1)} %fusion), kind=kOutput, calls=%fused_computation.5 | convolution fusion | flops 1109704704 | bytes 7077888 | tf_op jit(solution)/shard_map/dot_general | solution.py:93
  195.8 1.5 reshape.151
  197.4 9.3 %all-to-all-start.3 = ((bf16[32,12,2048]{2,1,0:T(8,128)(2,1)}), bf16[32,12,2048]{2,1,0:T(8,128)(2,1)S(1)}, u32[]{:S(2)}, u32[]{:S(2)}) async-start(bf16[32,12,2048]{2,1,0:T(8,128)(2,1)} %reshape.151), calls=%async_computation.3 | async-start | bytes 4194304 | tf_op jit(solution)/shard_map/all_to_all | solution.py:95
  208.6 1.3 copy.29
  213.3 17.8 %all-gather.8.cloned.1.call-done = bf16[512,2816]{0,1:T(8,128)(2,1)} async-done(((bf16[512,176]{0,1:T(8,128)(2,1)}), bf16[512,2816]{0,1:T(8,128)(2,1)}) %all-gather.8.cloned.1.call-update) | async-done | bytes 2883600 | tf_op jit(solution)/shard_map/all_gather | solution.py:107
  231.1 3.6 %fusion.22 = f32[512,128]{1,0:T(8,128)} fusion(bf16[512,2816]{0,1:T(8,128)(2,1)} %all-gather.8.cloned.1.call-done, bf16[2816,128]{1,0:T(8,128)(2,1)} %param.22), kind=kOutput, calls=%fused_computation.55 | convolution fusion | flops 369098752 | bytes 3866624 | tf_op jit(solution)/shard_map/dot_general | solution.py:106
  234.8 20.8 %all-to-all-done.3 = bf16[32,12,2048]{2,1,0:T(8,128)(2,1)S(1)} async-done(((bf16[32,12,2048]{2,1,0:T(8,128)(2,1)}), bf16[32,12,2048]{2,1,0:T(8,128)(2,1)S(1)}, u32[]{:S(2)}, u32[]{:S(2)}) %all-to-all-start.3) | async-done | bytes 1572896 | tf_op jit(solution)/shard_map/all_to_all | solution.py:95
  255.5 6.1 %all-to-all-start.4 = ((f32[16,32,128]{2,1,0:T(8,128)}), f32[16,32,128]{2,1,0:T(8,128)}, u32[]{:S(2)}, u32[]{:S(2)}) async-start(f32[16,32,128]{2,1,0:T(8,128)} %bitcast.65), calls=%async_computation.4 | async-start | bytes 524288 | tf_op jit(solution)/shard_map/all_to_all | solution.py:111
  263.0 2.5 reshape.152
  265.6 2.2 gather_fusion
  267.7 1.4 gather.7
  269.1 1.7 multiply_reduce_fusion
  270.8 2.7 all-to-all-done.4
  274.6 1.7 multiply_convert_fusion
  (72 shorter events, 16.2 us)
Async XLA Ops:
  6.5 118.2 %copy-start = (bf16[2048,2,176]{0,2,1:T(8,128)(2,1)S(1)}, bf16[2048,2,176]{0,2,1:T(8,128)(2,1)}, u32[]{:S(2)}) copy-start(bf16[2048,2,176]{0,2,1:T(8,128)(2,1)} %param.21) | copy-start | bytes 4325380
  6.5 118.2 %all-gather.6.cloned.1.call-start = ((), (), s32[]{:S(2)}) async-start(), calls=%async_computation.6 | async-start | bytes 2228224 | tf_op jit(solution)/shard_map/all_gather | solution.py:99
  7.8 62.8 %copy-start.5 = (bf16[2048,128]{1,0:T(8,128)(2,1)S(1)}, bf16[2048,128]{1,0:T(8,128)(2,1)}, u32[]{:S(2)}) copy-start(bf16[2048,128]{1,0:T(8,128)(2,1)} %param.14) | copy-start | bytes 1572868
  70.6 12.6 %copy-start.8 = (bf16[32,2048]{1,0:T(8,128)(2,1)S(1)}, bf16[32,2048]{1,0:T(8,128)(2,1)}, u32[]{:S(2)}) copy-start(bf16[32,2048]{1,0:T(8,128)(2,1)} %param.12) | copy-start | bytes 393220
  70.6 13.4 %copy-start.13 = (f32[2048]{0:T(1024)S(1)}, f32[2048]{0:T(1024)}, u32[]{:S(2)}) copy-start(f32[2048]{0:T(1024)} %param.15) | copy-start | bytes 24580
  70.6 14.3 %copy-start.7 = (bf16[1,704,128]{2,1,0:T(8,128)(2,1)S(1)}, bf16[1,704,128]{2,1,0:T(8,128)(2,1)}, u32[]{:S(2)}) copy-start(bf16[1,704,128]{2,1,0:T(8,128)(2,1)} %param.20) | copy-start | bytes 540676
  70.6 14.4 %copy-start.6 = (bf16[1,128,1408]{2,1,0:T(8,128)(2,1)S(1)}, bf16[1,128,1408]{2,1,0:T(8,128)(2,1)}, u32[]{:S(2)}) copy-start(bf16[1,128,1408]{2,1,0:T(8,128)(2,1)} %param.19) | copy-start | bytes 1081348
  71.3 14.6 %copy-start.10 = (s32[32,6]{0,1:T(8,128)S(1)}, s32[32,6]{0,1:T(8,128)}, u32[]{:S(2)}) copy-start(s32[32,6]{0,1:T(8,128)} %param.17) | copy-start | bytes 2308
  71.3 14.6 %copy-start.14 = (s32[32]{0:T(128)S(1)}, s32[32]{0:T(128)}, u32[]{:S(2)}) copy-start(s32[32]{0:T(128)} %param.18) | copy-start | bytes 388
  83.4 0.6 copy-start.2
  84.8 3.5 %copy-start.4 = (bf16[32,2048]{1,0:T(8,128)(2,1)S(1)}, bf16[32,2048]{1,0:T(8,128)(2,1)}, u32[]{:S(2)}) copy-start(bf16[32,2048]{1,0:T(8,128)(2,1)} %fusion.11) | copy-start | bytes 393220
  84.8 101.9 %all-gather.4.cloned.1.call-start = ((), (), s32[]{:S(2)}) async-start(), calls=%async_computation.5 | async-start | bytes 9469952 | tf_op jit(solution)/shard_map/all_gather | solution.py:28
  87.4 0.8 copy-start.11
  90.6 59.7 %all-to-all-start.2 = ((bf16[32,12,2048]{2,1,0:T(8,128)(2,1)}), bf16[32,12,2048]{2,1,0:T(8,128)(2,1)S(1)}, u32[]{:S(2)}, u32[]{:S(2)}) async-start(bf16[32,12,2048]{2,1,0:T(8,128)(2,1)} %reshape.147), calls=%async_computation.2 | async-start | bytes 4194304 | tf_op jit(solution)/shard_map/all_to_all | solution.py:88
  100.2 130.9 %all-gather.8.cloned.1.call-start = ((), (), s32[]{:S(2)}) async-start(), calls=%async_computation.7 | async-start | bytes 3063808 | tf_op jit(solution)/shard_map/all_gather | solution.py:107
  197.4 58.2 %all-to-all-start.3 = ((bf16[32,12,2048]{2,1,0:T(8,128)(2,1)}), bf16[32,12,2048]{2,1,0:T(8,128)(2,1)S(1)}, u32[]{:S(2)}, u32[]{:S(2)}) async-start(bf16[32,12,2048]{2,1,0:T(8,128)(2,1)} %reshape.151), calls=%async_computation.3 | async-start | bytes 4194304 | tf_op jit(solution)/shard_map/all_to_all | solution.py:95
  255.5 6.7 %copy-start.1 = (bf16[32,12,2048]{2,1,0:T(8,128)(2,1)}, bf16[32,12,2048]{2,1,0:T(8,128)(2,1)S(1)}, u32[]{:S(2)}) copy-start(bf16[32,12,2048]{2,1,0:T(8,128)(2,1)S(1)} %all-to-all-done.3) | copy-start | bytes 4718596
  255.5 18.0 %all-to-all-start.4 = ((f32[16,32,128]{2,1,0:T(8,128)}), f32[16,32,128]{2,1,0:T(8,128)}, u32[]{:S(2)}, u32[]{:S(2)}) async-start(f32[16,32,128]{2,1,0:T(8,128)} %bitcast.65), calls=%async_computation.4 | async-start | bytes 524288 | tf_op jit(solution)/shard_map/all_to_all | solution.py:111
  265.5 3.6 %copy-start.9 = (pred[32,6]{1,0:T(8,128)(4,1)S(1)}, pred[32,6]{1,0:T(8,128)(4,1)}, u32[]{:S(2)}) copy-start(pred[32,6]{1,0:T(8,128)(4,1)} %copy.29) | copy-start | bytes 580
  267.7 5.8 %copy-start.3 = (bf16[32,2048]{1,0:T(8,128)(2,1)S(1)}, bf16[32,2048]{1,0:T(8,128)(2,1)}, u32[]{:S(2)}) copy-start(bf16[32,2048]{1,0:T(8,128)(2,1)} %copy-done.2) | copy-start | bytes 393220
  267.7 6.9 %copy-start.12 = (f32[2048]{0:T(1024)S(1)}, f32[2048]{0:T(1024)}, u32[]{:S(2)}) copy-start(f32[2048]{0:T(1024)} %param.23) | copy-start | bytes 24580
Sparse Core Ops, SparseCore 0:
  84.9 39.7 all-gather.5
  126.8 59.8 all-gather.3
  188.9 42.1 all-gather.7
where the time goes:
time: 284 us; the launch traced here: 283 us
  waiting for transfers between devices  123 us (43%)
  blocking collectives  74.6 us (26%)
  starting transfers between devices  25.1 us (9%)
  matrix products  17.7 us (6%)
  local copies, waits for them, and re-layouts  16.8 us (6%)
  between operations  13.4 us (5%)
  other arithmetic  12.2 us (4%)
    all_to_all x1, blocking collectives, sent_to_all(): return lax.all_to_all(copies, axis, split_axis=0, concat_axis=0, tiled=True)  62.8 us
    all_gather x1, waiting for transfers between devices, turned_gather(): out = lax.all_gather(both, axis, axis=0, tiled=True)  35.1 us
    all_gather x1, waiting for transfers between devices, per_device(): lax.all_gather(normed, 'dp', axis=0, tiled=True)  24.4 us
    all_to_all x1, waiting for transfers between devices, per_device(): lax.all_to_all(outgoing, 'expert', split_axis=0, concat_axis=0, tiled=True)  22.2 us
    all_to_all x1, waiting for transfers between devices, per_device(): lax.all_to_all(result, 'expert', split_axis=0, concat_axis=0, tiled=True)  20.8 us
    all_gather x1, waiting for transfers between devices, per_device(): lax.all_gather(shared_hidden, 'dp', axis=1, tiled=True)  17.8 us
    all_to_all x1, blocking collectives, per_device(): lax.all_to_all(proj_cols, 'dp', split_axis=0, concat_axis=1, tiled=True)  11.9 us
    all_to_all x1, starting transfers between devices, per_device(): lax.all_to_all(outgoing, 'expert', split_axis=0, concat_axis=0, tiled=True)  9.67 us
  transfers between devices with their start and end apart: 6, of which 6 were waited for; matrix products, arithmetic and copies ran while one was open for 14% of the time, Pallas kernels for 0%

commit v1 on v0

--- a/solution.py
+++ b/solution.py
@@ -4,6 +4,13 @@
 from jax.sharding import PartitionSpec as P
 
 EPS = 1e-06
+
+
+def exchange_gather(x, axis, dim):
+    n_dev = lax.axis_size(axis)
+    blocks = jnp.stack([x for _ in range(n_dev)])
+    blocks = lax.all_to_all(blocks, axis, split_axis=0, concat_axis=0)
+    return jnp.concatenate(blocks, axis=dim)
 
 
 def in_order(blocks, dim):
@@ -104,9 +111,7 @@
         jnp.bfloat16
     )
     out_cols = jnp.dot(
-        lax.all_gather(shared_hidden, "dp", axis=1, tiled=True),
-        shared_down,
-        preferred_element_type=jnp.float32,
+        exchange_gather(shared_hidden, "dp", 1), shared_down, preferred_element_type=jnp.float32
     )
     shared_out = lax.all_to_all(out_cols, "dp", split_axis=0, concat_axis=1, tiled=True)
     back_rows = jnp.take(returned.reshape(experts * capacity, width), target, axis=0)

time: 284 us -> 346 us (1.22)
  waiting for transfers between devices: 123 us -> 161 us
  local copies, waits for them, and re-layouts: 16.8 us -> 35.6 us
  starting transfers between devices: 25.1 us -> 30.1 us
    all_gather x1, waiting for transfers between devices: 35.1 us -> 89 us  [turned_gather(): out = lax.all_gather(both, axis, axis=0, tiled=True)]
    all_gather x1 -> x0, waiting for transfers between devices: 17.8 us -> none  [per_device(): lax.all_gather(shared_hidden, 'dp', axis=1, tiled=True)]
    dot_general x0 -> x1, local copies, waits for them, and re-layouts: none -> 8.38 us  [per_device(): jnp.dot(exchange_gather(shared_hidden, 'dp', 1), shared_down, preferred_e...]
    reshape x0 -> x1, local copies, waits for them, and re-layouts: none -> 7.63 us  [exchange_gather(): return jnp.concatenate(blocks, axis=dim)]
    all_to_all x0 -> x1, starting transfers between devices: none -> 4.95 us  [exchange_gather(): blocks = lax.all_to_all(blocks, axis, split_axis=0, concat_axis=0)]
  transfers between devices with their start and end apart: 6 -> 6, of which waited for: 6 -> 5; matrix products, arithmetic and copies ran while one was open for 14% -> 17% of each run, Pallas kernels for 0% -> 0%
where the time goes in v1:
time: 346 us; the launch traced here: 345 us
  waiting for transfers between devices  161 us (47%)
  blocking collectives  74.6 us (22%)
  local copies, waits for them, and re-layouts  35.6 us (10%)
  starting transfers between devices  30.1 us (9%)
  matrix products  17.6 us (5%)
  between operations  13.7 us (4%)
  other arithmetic  12.1 us (3%)
    all_gather x1, waiting for transfers between devices, turned_gather(): out = lax.all_gather(both, axis, axis=0, tiled=True)  89 us
    all_to_all x1, blocking collectives, sent_to_all(): return lax.all_to_all(copies, axis, split_axis=0, concat_axis=0, tiled=True)  62.8 us
    all_gather x1, waiting for transfers between devices, per_device(): lax.all_gather(normed, 'dp', axis=0, tiled=True)  24.6 us
    all_to_all x1, waiting for transfers between devices, per_device(): lax.all_to_all(result, 'expert', split_axis=0, concat_axis=0, tiled=True)  22.6 us
    all_to_all x1, waiting for transfers between devices, per_device(): lax.all_to_all(outgoing, 'expert', split_axis=0, concat_axis=0, tiled=True)  22.1 us
    all_to_all x1, blocking collectives, per_device(): lax.all_to_all(proj_cols, 'dp', split_axis=0, concat_axis=1, tiled=True)  11.9 us
    all_to_all x1, starting transfers between devices, per_device(): lax.all_to_all(outgoing, 'expert', split_axis=0, concat_axis=0, tiled=True)  9.67 us
    all_to_all x1, starting transfers between devices, per_device(): lax.all_to_all(result, 'expert', split_axis=0, concat_axis=0, tiled=True)  9.55 us
  transfers between devices with their start and end apart: 6, of which 5 were waited for; matrix products, arithmetic and copies ran while one was open for 17% of the time, Pallas kernels for 0%

profile of v1, /device:TPU:1, one launch (start us, length us, event | category | flops | bytes accessed | tf_op | source)
XLA Modules:
  0.0 344.9 jit_solution(6094091933552486599)
XLA Ops:
  7.8 62.8 %all_to_all.49 = bf16[16,32,2048]{2,1,0:T(8,128)(2,1)S(1)} all-to-all(bf16[16,32,2048]{2,1,0:T(8,128)(2,1)S(1)} %broadcast_in_dim.50), channel_id=1, replica_groups=mesh['dp'=16,'expert'=32] {'dp'}, dimensions={0} | all-to-all | bytes 4194304 | tf_op jit(solution)/shard_map/all_to_all | solution.py:24
  71.4 11.9 %all_to_all.50 = bf16[16,32,128]{2,1,0:T(8,128)(2,1)S(1)} all-to-all(bf16[16,32,128]{2,1,0:T(8,128)(2,1)S(1)} %bitcast.67), channel_id=1, replica_groups=mesh['dp'=16,'expert'=32] {'dp'}, dimensions={0} | all-to-all | bytes 262144 | tf_op jit(solution)/shard_map/all_to_all | solution.py:73
  88.9 1.5 reshape.155
  90.4 9.7 %all-to-all-start.2 = ((bf16[32,12,2048]{2,1,0:T(8,128)(2,1)}), bf16[32,12,2048]{2,1,0:T(8,128)(2,1)S(1)}, u32[]{:S(2)}, u32[]{:S(2)}) async-start(bf16[32,12,2048]{2,1,0:T(8,128)(2,1)} %reshape.155), calls=%async_computation.2 | async-start | bytes 4194304 | tf_op jit(solution)/shard_map/all_to_all | solution.py:95
  100.1 24.6 %all-gather.5.cloned.1.call-done = bf16[512,2048]{1,0:T(8,128)(2,1)} async-done(((bf16[32,2048]{1,0:T(8,128)(2,1)}), bf16[512,2048]{1,0:T(8,128)(2,1)}) %all-gather.5.cloned.1.call-update) | async-done | bytes 2097168 | tf_op jit(solution)/shard_map/all_gather | solution.py:106
  124.7 2.5 fusion.23
  128.0 22.1 %all-to-all-done.2 = bf16[32,12,2048]{2,1,0:T(8,128)(2,1)S(1)} async-done(((bf16[32,12,2048]{2,1,0:T(8,128)(2,1)}), bf16[32,12,2048]{2,1,0:T(8,128)(2,1)S(1)}, u32[]{:S(2)}, u32[]{:S(2)}) %all-to-all-start.2) | async-done | bytes 1572896 | tf_op jit(solution)/shard_map/all_to_all | solution.py:95
  150.1 2.9 stack.2
  153.0 5.0 %all-to-all-start.4 = ((bf16[16,512,176]{1,2,0:T(8,128)(2,1)}), bf16[16,512,176]{1,2,0:T(8,128)(2,1)}, u32[]{:S(2)}, u32[]{:S(2)}) async-start(bf16[16,512,176]{1,2,0:T(8,128)(2,1)} %stack.2), calls=%async_computation.4 | async-start | bytes 5767168 | tf_op jit(solution)/shard_map/all_to_all | solution.py:12
  159.3 89.0 %all-gather.3.cloned.1.call-done = bf16[2048,2112]{1,0:T(8,128)(2,1)} async-done(((bf16[128,2112]{1,0:T(8,128)(2,1)}), bf16[2048,2112]{1,0:T(8,128)(2,1)}) %all-gather.3.cloned.1.call-update) | async-done | bytes 8650768 | tf_op jit(solution)/shard_map/all_gather | solution.py:35
  248.3 5.7 %fusion = f32[384,1408]{1,0:T(8,128)S(1)} fusion(bf16[384,2048]{1,0:T(8,128)(2,1)} %reshape.156, bf16[2048,2112]{1,0:T(8,128)(2,1)} %all-gather.3.cloned.1.call-done), kind=kOutput, calls=%fused_computation.1 | convolution fusion | flops 2214592512 | bytes 9502720 | tf_op jit(solution)/shard_map/dot_general | solution.py:98
  254.0 3.3 fusion.3
  257.3 1.5 reshape.159
  258.9 9.5 %all-to-all-start.3 = ((bf16[32,12,2048]{2,1,0:T(8,128)(2,1)}), bf16[32,12,2048]{2,1,0:T(8,128)(2,1)S(1)}, u32[]{:S(2)}, u32[]{:S(2)}) async-start(bf16[32,12,2048]{2,1,0:T(8,128)(2,1)} %reshape.159), calls=%async_computation.3 | async-start | bytes 4194304 | tf_op jit(solution)/shard_map/all_to_all | solution.py:102
  275.1 7.6 %copy.40 = bf16[512,16,176]{2,1,0:T(8,128)(2,1)} copy(bf16[512,16,176]{0,2,1:T(8,128)(2,1)} %bitcast.13) | data formatting | bytes 5767168 | tf_op jit(solution)/shard_map/reshape | solution.py:13
  282.7 8.4 %dot_general.29 = bf16[16,32,2816]{2,1,0:T(8,128)(2,1)} reshape(bf16[512,16,176]{2,1,0:T(8,128)(2,1)} %copy.40) | data formatting | bytes 5767168 | tf_op jit(solution)/shard_map/dot_general | solution.py:113
  291.1 3.6 %fusion.5 = f32[16,32,128]{2,1,0:T(8,128)} fusion(bf16[16,32,2816]{2,1,0:T(8,128)(2,1)} %dot_general.29, bf16[2816,128]{1,0:T(8,128)(2,1)} %param.22), kind=kOutput, calls=%fused_computation.11 | convolution fusion | flops 369098752 | bytes 3866624 | tf_op jit(solution)/shard_map/dot_general | solution.py:113
  294.7 22.6 %all-to-all-done.3 = bf16[32,12,2048]{2,1,0:T(8,128)(2,1)S(1)} async-done(((bf16[32,12,2048]{2,1,0:T(8,128)(2,1)}), bf16[32,12,2048]{2,1,0:T(8,128)(2,1)S(1)}, u32[]{:S(2)}, u32[]{:S(2)}) %all-to-all-start.3) | async-done | bytes 1572896 | tf_op jit(solution)/shard_map/all_to_all | solution.py:102
  317.3 5.9 %all-to-all-start.5 = ((f32[16,32,128]{2,1,0:T(8,128)}), f32[16,32,128]{2,1,0:T(8,128)}, u32[]{:S(2)}, u32[]{:S(2)}) async-start(f32[16,32,128]{2,1,0:T(8,128)} %fusion.5), calls=%async_computation.5 | async-start | bytes 524288 | tf_op jit(solution)/shard_map/all_to_all | solution.py:116
  324.7 2.5 reshape.160
  327.2 2.2 gather_fusion
  330.7 1.7 multiply_reduce_fusion
  332.4 2.8 all-to-all-done.5
  336.4 1.7 multiply_convert_fusion
  (74 shorter events, 20.2 us)
Async XLA Ops:
  6.5 118.1 %copy-start = (bf16[2048,2,176]{0,2,1:T(8,128)(2,1)S(1)}, bf16[2048,2,176]{0,2,1:T(8,128)(2,1)}, u32[]{:S(2)}) copy-start(bf16[2048,2,176]{0,2,1:T(8,128)(2,1)} %param.21) | copy-start | bytes 4325380
  6.5 118.1 %all-gather.5.cloned.1.call-start = ((), (), s32[]{:S(2)}) async-start(), calls=%async_computation.7 | async-start | bytes 2228224 | tf_op jit(solution)/shard_map/all_gather | solution.py:106
  7.8 62.8 %copy-start.5 = (bf16[2048,128]{1,0:T(8,128)(2,1)S(1)}, bf16[2048,128]{1,0:T(8,128)(2,1)}, u32[]{:S(2)}) copy-start(bf16[2048,128]{1,0:T(8,128)(2,1)} %param.14) | copy-start | bytes 1572868
  70.6 12.6 %copy-start.8 = (bf16[32,2048]{1,0:T(8,128)(2,1)S(1)}, bf16[32,2048]{1,0:T(8,128)(2,1)}, u32[]{:S(2)}) copy-start(bf16[32,2048]{1,0:T(8,128)(2,1)} %param.12) | copy-start | bytes 393220
  70.6 13.4 %copy-start.13 = (f32[2048]{0:T(1024)S(1)}, f32[2048]{0:T(1024)}, u32[]{:S(2)}) copy-start(f32[2048]{0:T(1024)} %param.15) | copy-start | bytes 24580
  70.6 14.3 %copy-start.7 = (bf16[1,704,128]{2,1,0:T(8,128)(2,1)S(1)}, bf16[1,704,128]{2,1,0:T(8,128)(2,1)}, u32[]{:S(2)}) copy-start(bf16[1,704,128]{2,1,0:T(8,128)(2,1)} %param.20) | copy-start | bytes 540676
  70.6 14.4 %copy-start.6 = (bf16[1,128,1408]{2,1,0:T(8,128)(2,1)S(1)}, bf16[1,128,1408]{2,1,0:T(8,128)(2,1)}, u32[]{:S(2)}) copy-start(bf16[1,128,1408]{2,1,0:T(8,128)(2,1)} %param.19) | copy-start | bytes 1081348
  71.3 14.6 %copy-start.10 = (s32[32,6]{0,1:T(8,128)S(1)}, s32[32,6]{0,1:T(8,128)}, u32[]{:S(2)}) copy-start(s32[32,6]{0,1:T(8,128)} %param.17) | copy-start | bytes 2308
  71.3 14.6 %copy-start.14 = (s32[32]{0:T(128)S(1)}, s32[32]{0:T(128)}, u32[]{:S(2)}) copy-start(s32[32]{0:T(128)} %param.18) | copy-start | bytes 388
  83.4 0.6 copy-start.2
  84.8 3.5 %copy-start.4 = (bf16[32,2048]{1,0:T(8,128)(2,1)S(1)}, bf16[32,2048]{1,0:T(8,128)(2,1)}, u32[]{:S(2)}) copy-start(bf16[32,2048]{1,0:T(8,128)(2,1)} %fusion.13) | copy-start | bytes 393220
  84.8 163.5 %all-gather.3.cloned.1.call-start = ((), (), s32[]{:S(2)}) async-start(), calls=%async_computation.6 | async-start | bytes 9469952 | tf_op jit(solution)/shard_map/all_gather | solution.py:35
  87.4 0.8 copy-start.11
  90.4 59.7 %all-to-all-start.2 = ((bf16[32,12,2048]{2,1,0:T(8,128)(2,1)}), bf16[32,12,2048]{2,1,0:T(8,128)(2,1)S(1)}, u32[]{:S(2)}, u32[]{:S(2)}) async-start(bf16[32,12,2048]{2,1,0:T(8,128)(2,1)} %reshape.155), calls=%async_computation.2 | async-start | bytes 4194304 | tf_op jit(solution)/shard_map/all_to_all | solution.py:95
  153.0 105.9 %all-to-all-start.4 = ((bf16[16,512,176]{1,2,0:T(8,128)(2,1)}), bf16[16,512,176]{1,2,0:T(8,128)(2,1)}, u32[]{:S(2)}, u32[]{:S(2)}) async-start(bf16[16,512,176]{1,2,0:T(8,128)(2,1)} %stack.2), calls=%async_computation.4 | async-start | bytes 5767168 | tf_op jit(solution)/shard_map/all_to_all | solution.py:12
  258.9 58.5 %all-to-all-start.3 = ((bf16[32,12,2048]{2,1,0:T(8,128)(2,1)}), bf16[32,12,2048]{2,1,0:T(8,128)(2,1)S(1)}, u32[]{:S(2)}, u32[]{:S(2)}) async-start(bf16[32,12,2048]{2,1,0:T(8,128)(2,1)} %reshape.159), calls=%async_computation.3 | async-start | bytes 4194304 | tf_op jit(solution)/shard_map/all_to_all | solution.py:102
  317.3 6.6 %copy-start.1 = (bf16[32,12,2048]{2,1,0:T(8,128)(2,1)}, bf16[32,12,2048]{2,1,0:T(8,128)(2,1)S(1)}, u32[]{:S(2)}) copy-start(bf16[32,12,2048]{2,1,0:T(8,128)(2,1)S(1)} %all-to-all-done.3) | copy-start | bytes 4718596
  317.3 17.9 %all-to-all-start.5 = ((f32[16,32,128]{2,1,0:T(8,128)}), f32[16,32,128]{2,1,0:T(8,128)}, u32[]{:S(2)}, u32[]{:S(2)}) async-start(f32[16,32,128]{2,1,0:T(8,128)} %fusion.5), calls=%async_computation.5 | async-start | bytes 524288 | tf_op jit(solution)/shard_map/all_to_all | solution.py:116
  327.2 3.6 %copy-start.9 = (pred[32,6]{1,0:T(8,128)(4,1)S(1)}, pred[32,6]{1,0:T(8,128)(4,1)}, u32[]{:S(2)}) copy-start(pred[32,6]{1,0:T(8,128)(4,1)} %copy.37) | copy-start | bytes 580
  329.3 5.9 %copy-start.3 = (bf16[32,2048]{1,0:T(8,128)(2,1)S(1)}, bf16[32,2048]{1,0:T(8,128)(2,1)}, u32[]{:S(2)}) copy-start(bf16[32,2048]{1,0:T(8,128)(2,1)} %copy-done.2) | copy-start | bytes 393220
  329.3 7.0 %copy-start.12 = (f32[2048]{0:T(1024)S(1)}, f32[2048]{0:T(1024)}, u32[]{:S(2)}) copy-start(f32[2048]{0:T(1024)} %param.23) | copy-start | bytes 24580
Sparse Core Ops, SparseCore 0:
  84.9 39.6 all-gather.4
  126.8 121.4 all-gather.2
